TPU v7x, 256 devices: a whole 4x4x8 slice. The times are simulated.
256 devices in a mesh: tiles: 64 (over y, z, core), cols: 4 (over x).
Axes of the slice: x: 4, y: 4, z: 8, core: 2. Of those that a mesh axis runs over, the one named last changes fastest.
Arguments:
- cov_blocks: bfloat16 [1024, 8, 256, 256], P('tiles', None, 'cols'), may hold values from -1 to 5, as said below
- neighbours: int32 [1024, 8], P('tiles'), may hold values from 0 to 1023, as said below
- voxel_mask: int32 [1024, 256], P('tiles', 'cols'), may hold values 0 or 1
- start_block: bfloat16 [128, 1024, 256], P('cols', 'tiles'), may hold values from -6 to 6
- overdensity: float32 [1024, 256], P('tiles', 'cols'), may hold values from -12 to 12
Outputs:
- basis_next: bfloat16 [128, 1024, 256], P('cols', 'tiles')
- coeffs: float32 [3, 128], replicated
Inputs may be any that keep to these rules, and one draw needn't show every extreme that they name: Slot 0 names the tile itself. Every other entry names another tile at most 3 away, counting cyclically (tile 1024 - 1 is next to tile 0), and some entry is exactly 3 away. If neighbours[i, k] = j then neighbours[j, k] = i. cov_blocks[j, k] is the transpose of cov_blocks[i, k] where neighbours[i, k] = j; the blocks of slot 0 are symmetric.
All inputs are finite; a program needn't handle non-finite values. No bound on the sum of `voxel_mask` on one device may be relied on, other than what follows from the above.
Results may differ from a plain program's by a relative error of at most 0.01.
The roundings to bfloat16 on the way count: a program that leaves them out, or rounds other values in their place, can miss the bound.
Values may be sent and summed in bfloat16 or wider, within the bound.
No kernel may reach another device: no remote copies, remote signals or barrier semaphores. Data moves between devices by JAX's collectives and lax.ppermute only.
A program may use at most 64 MiB of HBM per device.

v0:
```python
import math
import jax
import jax.numpy as jnp
from jax import lax
from jax.sharding import PartitionSpec as P

REACH = 3


def with_halo(cells, sides, width):
    for axis, dim in sides:
        count = lax.axis_size(axis)
        head = lax.slice_in_dim(cells, 0, width, axis=dim)
        tail = lax.slice_in_dim(cells, cells.shape[dim] - width, cells.shape[dim], axis=dim)
        cells = jnp.concatenate(
            [
                lax.ppermute(tail, axis, [(i, (i + 1) % count) for i in range(count)]),
                cells,
                lax.ppermute(head, axis, [((i + 1) % count, i) for i in range(count)]),
            ],
            axis=dim,
        )
    return cells


def pair_step(x, axis, count, stride):
    perm = [(i, i ^ stride) for i in range(count)]
    return x + lax.ppermute(x, axis, perm)


def group_step(x, axis, count, stride, size):
    me = lax.axis_index(axis) // stride % size
    vals = [x]
    for shift in range(1, size):
        perm = []
        for i in range(count):
            digit = i // stride % size
            perm.append((i, i + ((digit + shift) % size - digit) * stride))
        vals.append(lax.ppermute(x, axis, perm))
    ordered = jnp.take(jnp.stack(vals), (me - jnp.arange(size)) % size, axis=0)
    return jnp.sum(ordered, axis=0)


def plan_of(count):
    stages = []
    stride = 1
    pair_next = count > 4
    while stride < count:
        if not pair_next and count // stride >= 4:
            stages.append(("group", stride, 4))
            stride *= 4
        else:
            stages.append(("pair", stride, 2))
            stride *= 2
        pair_next = not pair_next
    return stages


def all_sum(x, axes=("cols", "tiles")):
    for axis in axes:
        count = lax.axis_size(axis)
        if count & count - 1:
            x = lax.psum(x, axis)
            continue
        for kind, stride, size in plan_of(count):
            if kind == "pair":
                x = pair_step(x, axis, count, stride)
            else:
                x = group_step(x, axis, count, stride, size)
    return x


def orthonormal(work):
    gram = all_sum(jnp.dot(work, work.T, preferred_element_type=jnp.float32))
    lower = jnp.linalg.cholesky(gram)
    identity = jnp.eye(work.shape[0], dtype=jnp.float32)
    inverse = jax.scipy.linalg.solve_triangular(lower, identity, lower=True).astype(jnp.bfloat16)
    return jnp.dot(inverse, work, preferred_element_type=jnp.float32)


def projection(basis_flat, density):
    return jnp.sum(basis_flat.astype(jnp.float32) * density[None, :], axis=1)


def fold_slots(total, piece, cov_blocks, local_index):
    for slot in range(cov_blocks.shape[1]):
        picked = jnp.take(piece, local_index[:, slot], axis=1)
        blocks = cov_blocks[:, slot]
        total = total + jnp.einsum(
            "iuv,biv->biu", blocks, picked, preferred_element_type=jnp.float32
        )
    return total


def local(cov_blocks, neighbours, voxel_mask, start_block, overdensity):
    tiles_here = neighbours.shape[0]
    voxels_here = voxel_mask.shape[1]
    voxels_all = cov_blocks.shape[3]
    cycle_size = tiles_here * lax.axis_size("tiles")
    first_tile = lax.axis_index("tiles") * tiles_here
    local_index = jnp.mod(neighbours - first_tile + REACH, cycle_size)
    mask_values = voxel_mask.astype(jnp.float32)
    density = overdensity.reshape(-1)
    start_cube = lax.all_to_all(start_block, "cols", split_axis=2, concat_axis=0, tiled=True)
    count = start_cube.shape[0]
    start_flat = (
        (start_cube.astype(jnp.float32) * mask_values[None]).astype(jnp.bfloat16).reshape(count, -1)
    )
    basis_now = orthonormal(start_flat).astype(jnp.bfloat16)
    basis_old = None
    found = []
    pending = projection(basis_now, density)
    rotated = None
    for lanczos_round in range(2):
        image_count = basis_now.shape[0]
        basis_cube = basis_now.reshape(image_count, tiles_here, voxels_here)
        empty = jnp.zeros((image_count, tiles_here, voxels_here), jnp.float32)
        gathered = lax.all_gather(basis_cube, "cols", axis=2, tiled=True)
        padded = with_halo(gathered, (("tiles", 1),), REACH)
        total = fold_slots(empty, padded, cov_blocks, local_index)
        image = (total * mask_values[None]).astype(jnp.bfloat16).reshape(image_count, -1)
        if basis_old is None:
            stacked = basis_now
        else:
            stacked = jnp.concatenate([basis_now, basis_old], axis=0)
        local_sums = jnp.dot(stacked, image.T, preferred_element_type=jnp.float32)
        sums = all_sum(jnp.concatenate([local_sums, pending[None]], axis=0))
        found.append(sums[-1])
        along = sums[:count].astype(jnp.bfloat16)
        resid = image.astype(jnp.float32) - jnp.dot(
            along.T, basis_now, preferred_element_type=jnp.float32
        )
        if basis_old is not None:
            back = sums[count : 2 * count].astype(jnp.bfloat16)
            resid = resid - jnp.dot(back.T, basis_old, preferred_element_type=jnp.float32)
        rotated = orthonormal(resid.astype(jnp.bfloat16))
        basis_old, basis_now = (basis_now, rotated.astype(jnp.bfloat16))
        pending = projection(basis_now, density)
    found.append(all_sum(pending))
    coeffs = jnp.stack(found)
    scaled = (rotated * math.sqrt(cycle_size * voxels_all)).astype(jnp.bfloat16)
    scaled = scaled.reshape(count, tiles_here, voxels_here)
    basis_next = lax.all_to_all(scaled, "cols", split_axis=0, concat_axis=2, tiled=True)
    return (basis_next, coeffs)


def solution(mesh):
    return jax.shard_map(
        local,
        mesh=mesh,
        in_specs=(
            P("tiles", None, "cols", None),
            P("tiles", None),
            P("tiles", "cols"),
            P("cols", "tiles", None),
            P("tiles", "cols"),
        ),
        out_specs=(P("cols", "tiles", None), P()),
        check_vma=False,
    )
```

profile of v0, /device:TPU:8, one launch (start us, length us, event | category | flops | bytes accessed | tf_op | source)
XLA Modules:
  0.0 462.4 jit_solution(13479169176730320562)
XLA Ops:
  11.2 4.3 all-to-all-start
  17.1 5.1 %all-to-all-done = bf16[4,2,16384]{2,1,0:T(2,128)(2,1)S(1)} async-done(((bf16[4,2,16384]{2,1,0:T(2,128)(2,1)}), bf16[4,2,16384]{2,1,0:T(2,128)(2,1)S(1)}, u32[]{:S(2)}, u32[]{:S(2)}) %all-to-all-start) | async-done | bytes 262176 | tf_op jit(solution)/shard_map/all_to_all | solution.py:104
  35.3 3.3 collective-permute-start.5
  44.5 5.8 %collective-permute-start.7 = (f32[128,128]{1,0:T(8,128)S(1)}, f32[128,128]{1,0:T(8,128)S(1)}, u32[]{:S(2)}, u32[]{:S(2)}) collective-permute-start(f32[128,128]{1,0:T(8,128)S(1)} %select_reduce_fusion.13), channel_id=1, source_target_pairs={{0,32},{4,36},{8,40},{12,44},{16,48},{20,52},{24,56},{28,60},{32,0... | collective-permute-start | bytes 196616 | tf_op jit(solution)/shard_map/ppermute | solution.py:28
  61.3 11.7 %cholesky.59 = f32[128,128]{1,0:T(8,128)S(1)} custom-call(f32[128,128]{1,0:T(8,128)S(1)} %fusion.122), custom_call_target="Cholesky" | custom-call | tf_op jit(solution)/shard_map/jit(cholesky)/cholesky | solution.py:75
  74.3 9.8 %custom-call.7 = f32[1,128,128]{1,2,0:T(8,128)S(1)} custom-call(f32[1,128,128]{2,1,0:T(8,128)S(1)} %fusion.114), custom_call_target="InvertDiagBlocksLowerTriangular" | custom-call | tf_op jit(solution)/shard_map/jit(_solve_triangular)/triangular_solve | solution.py:77
  85.9 29.2 %all-gather.3.cloned.1.call-done = bf16[128,16,256]{0,1,2:T(8,128)(2,1)} async-done(((bf16[128,16,64]{0,1,2:T(8,128)(2,1)}), bf16[128,16,256]{0,1,2:T(8,128)(2,1)}) %all-gather.3.cloned.1.call-update) | async-done | bytes 1048592 | tf_op jit(solution)/shard_map/all_gather | solution.py:118
  116.9 4.0 collective-permute-start.12
  154.9 4.1 collective-permute-start.18
  165.2 4.1 collective-permute-start.20
  169.3 4.9 %collective-permute-done.20 = f32[129,128]{1,0:T(8,128)S(1)} collective-permute-done((f32[129,128]{1,0:T(8,128)S(1)}, f32[129,128]{1,0:T(8,128)S(1)}, u32[]{:S(2)}, u32[]{:S(2)}) %collective-permute-start.20) | collective-permute-done | bytes 66080 | tf_op jit(solution)/shard_map/ppermute | solution.py:28
  203.9 3.9 collective-permute-start.31
  207.8 5.1 %collective-permute-done.31 = f32[128,128]{1,0:T(8,128)S(1)} collective-permute-done((f32[128,128]{1,0:T(8,128)S(1)}, f32[128,128]{1,0:T(8,128)S(1)}, u32[]{:S(2)}, u32[]{:S(2)}) %collective-permute-start.31) | collective-permute-done | bytes 65568 | tf_op jit(solution)/shard_map/ppermute | solution.py:28
  222.2 11.7 %cholesky.70 = f32[128,128]{1,0:T(8,128)S(1)} custom-call(f32[128,128]{1,0:T(8,128)S(1)} %fusion.120), custom_call_target="Cholesky" | custom-call | tf_op jit(solution)/shard_map/jit(cholesky)/cholesky | solution.py:75
  235.3 9.8 %custom-call.8 = f32[1,128,128]{1,2,0:T(8,128)S(1)} custom-call(f32[1,128,128]{2,1,0:T(8,128)S(1)} %fusion.115), custom_call_target="InvertDiagBlocksLowerTriangular" | custom-call | tf_op jit(solution)/shard_map/jit(_solve_triangular)/triangular_solve | solution.py:77
  246.8 24.3 %all-gather.5.cloned.1.call-done = bf16[128,16,256]{0,1,2:T(8,128)(2,1)} async-done(((bf16[128,16,64]{0,1,2:T(8,128)(2,1)}), bf16[128,16,256]{0,1,2:T(8,128)(2,1)}) %all-gather.5.cloned.1.call-update) | async-done | bytes 1048592 | tf_op jit(solution)/shard_map/all_gather | solution.py:118
  272.8 4.0 collective-permute-start.36
  276.9 3.2 collective-permute-done.35
  306.0 4.9 %collective-permute-done.37 = f32[257,128]{1,0:T(8,128)S(1)} collective-permute-done((f32[257,128]{1,0:T(8,128)S(1)}, f32[257,128]{1,0:T(8,128)S(1)}, u32[]{:S(2)}, u32[]{:S(2)}) %collective-permute-start.37) | collective-permute-done | bytes 131616 | tf_op jit(solution)/shard_map/ppermute | solution.py:39
  317.8 4.3 collective-permute-done.41
  322.1 4.9 %collective-permute-done.42 = f32[257,128]{1,0:T(8,128)S(1)} collective-permute-done((f32[257,128]{1,0:T(8,128)S(1)}, f32[257,128]{1,0:T(8,128)S(1)}, u32[]{:S(2)}, u32[]{:S(2)}) %collective-permute-start.42) | collective-permute-done | bytes 131616 | tf_op jit(solution)/shard_map/ppermute | solution.py:39
  327.8 5.0 %collective-permute-start.44 = (f32[257,128]{1,0:T(8,128)S(1)}, f32[257,128]{1,0:T(8,128)S(1)}, u32[]{:S(2)}, u32[]{:S(2)}) collective-permute-start(f32[257,128]{1,0:T(8,128)S(1)} %select_reduce_fusion.1), channel_id=1, source_target_pairs={{0,32},{4,36},{8,40},{12,44},{16,48},{20,52},{24,56},{28,60},{32,0... | collective-permute-start | bytes 394760 | tf_op jit(solution)/shard_map/ppermute | solution.py:28
  332.8 4.1 collective-permute-done.44
  358.6 6.5 %collective-permute-start.52 = (f32[128,128]{1,0:T(8,128)S(1)}, f32[128,128]{1,0:T(8,128)S(1)}, u32[]{:S(2)}, u32[]{:S(2)}) collective-permute-start(f32[128,128]{1,0:T(8,128)S(1)} %add.231), channel_id=1, source_target_pairs={{0,8},{4,12},{8,16},{12,20},{16,24},{20,28},{24,0},{28,4},{32,40},... | collective-permute-start | bytes 196616 | tf_op jit(solution)/shard_map/ppermute | solution.py:39
  367.6 3.6 collective-permute-done.53
  371.9 4.2 collective-permute-start.55
  376.1 4.0 collective-permute-done.55
  388.5 11.7 %cholesky.81 = f32[128,128]{1,0:T(8,128)S(1)} custom-call(f32[128,128]{1,0:T(8,128)S(1)} %fusion.118), custom_call_target="Cholesky" | custom-call | tf_op jit(solution)/shard_map/jit(cholesky)/cholesky | solution.py:75
  401.5 9.8 %custom-call.9 = f32[1,128,128]{1,2,0:T(8,128)S(1)} custom-call(f32[1,128,128]{2,1,0:T(8,128)S(1)} %fusion.116), custom_call_target="InvertDiagBlocksLowerTriangular" | custom-call | tf_op jit(solution)/shard_map/jit(_solve_triangular)/triangular_solve | solution.py:77
  428.3 4.9 %collective-permute-start.66 = (f32[128]{0:T(128)S(1)}, f32[128]{0:T(128)S(1)}, u32[]{:S(2)}, u32[]{:S(2)}) collective-permute-start(f32[128]{0:T(128)S(1)} %select_reduce_fusion.17), channel_id=1, source_target_pairs={{0,32},{4,36},{8,40},{12,44},{16,48},{20,52},{24,56},{28,60},{32,0... | collective-permute-start | bytes 1544 | tf_op jit(solution)/shard_map/ppermute | solution.py:28
  443.0 3.9 all-to-all-start.1
  448.2 5.4 %all-to-all-done.1 = bf16[4,2,16384]{2,1,0:T(2,128)(2,1)S(1)} async-done(((bf16[4,2,16384]{2,1,0:T(2,128)(2,1)}), bf16[4,2,16384]{2,1,0:T(2,128)(2,1)S(1)}, u32[]{:S(2)}, u32[]{:S(2)}) %all-to-all-start.1) | async-done | bytes 262176 | tf_op jit(solution)/shard_map/all_to_all | solution.py:143
  (325 shorter events, 221.6 us)
Async XLA Ops:
  11.2 11.0 %all-to-all-start = ((bf16[4,2,16384]{2,1,0:T(2,128)(2,1)}), bf16[4,2,16384]{2,1,0:T(2,128)(2,1)S(1)}, u32[]{:S(2)}, u32[]{:S(2)}) async-start(bf16[4,2,16384]{2,1,0:T(2,128)(2,1)} %reshape.448), calls=%async_computation | async-start | bytes 524288 | tf_op jit(solution)/shard_map/all_to_all | solution.py:104
  15.5 99.6 %all-gather.3.cloned.1.call-start = ((), (), s32[]{:S(2)}) async-start(), calls=%async_computation.2 | async-start | bytes 1310720 | tf_op jit(solution)/shard_map/all_gather | solution.py:118
  33.4 7.6 %collective-permute-start.4 = (f32[128,128]{1,0:T(8,128)S(1)}, f32[128,128]{1,0:T(8,128)S(1)}, u32[]{:S(2)}, u32[]{:S(2)}) collective-permute-start(f32[128,128]{1,0:T(8,128)S(1)} %add.200), channel_id=1, source_target_pairs={{0,8},{4,12},{8,16},{12,20},{16,24},{20,28},{24,0},{28,4},{32,40},... | collective-permute-start | bytes 196616 | tf_op jit(solution)/shard_map/ppermute | solution.py:39
  35.3 8.0 %collective-permute-start.5 = (f32[128,128]{1,0:T(8,128)S(1)}, f32[128,128]{1,0:T(8,128)S(1)}, u32[]{:S(2)}, u32[]{:S(2)}) collective-permute-start(f32[128,128]{1,0:T(8,128)S(1)} %add.200), channel_id=1, source_target_pairs={{0,16},{4,20},{8,24},{12,28},{16,0},{20,4},{24,8},{28,12},{32,48},... | collective-permute-start | bytes 196616 | tf_op jit(solution)/shard_map/ppermute | solution.py:39
  44.5 8.3 %collective-permute-start.7 = (f32[128,128]{1,0:T(8,128)S(1)}, f32[128,128]{1,0:T(8,128)S(1)}, u32[]{:S(2)}, u32[]{:S(2)}) collective-permute-start(f32[128,128]{1,0:T(8,128)S(1)} %select_reduce_fusion.13), channel_id=1, source_target_pairs={{0,32},{4,36},{8,40},{12,44},{16,48},{20,52},{24,56},{28,60},{32,0... | collective-permute-start | bytes 196616 | tf_op jit(solution)/shard_map/ppermute | solution.py:28
  85.8 185.3 %all-gather.5.cloned.1.call-start = ((), (), s32[]{:S(2)}) async-start(), calls=%async_computation.3 | async-start | bytes 1310720 | tf_op jit(solution)/shard_map/all_gather | solution.py:118
  116.8 7.3 %collective-permute-start.11 = (bf16[128,3,256]{2,0,1:T(8,128)(2,1)S(1)}, bf16[128,3,256]{2,0,1:T(8,128)(2,1)S(1)}, u32[]{:S(2)}, u32[]{:S(2)}) collective-permute-start(bf16[128,3,256]{2,0,1:T(8,128)(2,1)S(1)} %get-tuple-element.27), channel_id=1, source_target_pairs={{0,4},{4,8},{8,12},{12,16},{16,20},{20,24},{24,28},{28,32},{32,36}... | collective-permute-start | bytes 589832 | tf_op jit(solution)/shard_map/ppermute | solution.py:17
  116.9 7.2 %collective-permute-start.12 = (bf16[128,3,256]{2,0,1:T(8,128)(2,1)S(1)}, bf16[128,3,256]{2,0,1:T(8,128)(2,1)S(1)}, u32[]{:S(2)}, u32[]{:S(2)}) collective-permute-start(bf16[128,3,256]{2,0,1:T(8,128)(2,1)S(1)} %get-tuple-element.28), channel_id=1, source_target_pairs={{4,0},{8,4},{12,8},{16,12},{20,16},{24,20},{28,24},{32,28},{36,32}... | collective-permute-start | bytes 589832 | tf_op jit(solution)/shard_map/ppermute | solution.py:19
  145.2 6.9 %collective-permute-start.13 = (f32[129,128]{1,0:T(8,128)S(1)}, f32[129,128]{1,0:T(8,128)S(1)}, u32[]{:S(2)}, u32[]{:S(2)}) collective-permute-start(f32[129,128]{1,0:T(8,128)S(1)} %get-tuple-element.34), channel_id=1, source_target_pairs={{0,1},{1,2},{2,3},{3,0},{4,5},{5,6},{6,7},{7,4},{8,9},{9,10},{10,1... | collective-permute-start | bytes 198152 | tf_op jit(solution)/shard_map/ppermute | solution.py:39
  154.7 7.0 %collective-permute-start.17 = (f32[129,128]{1,0:T(8,128)S(1)}, f32[129,128]{1,0:T(8,128)S(1)}, u32[]{:S(2)}, u32[]{:S(2)}) collective-permute-start(f32[129,128]{1,0:T(8,128)S(1)} %add.217), channel_id=1, source_target_pairs={{0,8},{4,12},{8,16},{12,20},{16,24},{20,28},{24,0},{28,4},{32,40},... | collective-permute-start | bytes 198152 | tf_op jit(solution)/shard_map/ppermute | solution.py:39
  154.9 9.3 %collective-permute-start.18 = (f32[129,128]{1,0:T(8,128)S(1)}, f32[129,128]{1,0:T(8,128)S(1)}, u32[]{:S(2)}, u32[]{:S(2)}) collective-permute-start(f32[129,128]{1,0:T(8,128)S(1)} %add.217), channel_id=1, source_target_pairs={{0,16},{4,20},{8,24},{12,28},{16,0},{20,4},{24,8},{28,12},{32,48},... | collective-permute-start | bytes 198152 | tf_op jit(solution)/shard_map/ppermute | solution.py:39
  165.2 9.0 %collective-permute-start.20 = (f32[129,128]{1,0:T(8,128)S(1)}, f32[129,128]{1,0:T(8,128)S(1)}, u32[]{:S(2)}, u32[]{:S(2)}) collective-permute-start(f32[129,128]{1,0:T(8,128)S(1)} %select_reduce_fusion.4), channel_id=1, source_target_pairs={{0,32},{4,36},{8,40},{12,44},{16,48},{20,52},{24,56},{28,60},{32,0... | collective-permute-start | bytes 198152 | tf_op jit(solution)/shard_map/ppermute | solution.py:28
  194.3 6.9 %collective-permute-start.28 = (f32[128,128]{1,0:T(8,128)S(1)}, f32[128,128]{1,0:T(8,128)S(1)}, u32[]{:S(2)}, u32[]{:S(2)}) collective-permute-start(f32[128,128]{1,0:T(8,128)S(1)} %add.219), channel_id=1, source_target_pairs={{0,8},{4,12},{8,16},{12,20},{16,24},{20,28},{24,0},{28,4},{32,40},... | collective-permute-start | bytes 196616 | tf_op jit(solution)/shard_map/ppermute | solution.py:39
  195.8 7.4 %collective-permute-start.29 = (f32[128,128]{1,0:T(8,128)S(1)}, f32[128,128]{1,0:T(8,128)S(1)}, u32[]{:S(2)}, u32[]{:S(2)}) collective-permute-start(f32[128,128]{1,0:T(8,128)S(1)} %add.219), channel_id=1, source_target_pairs={{0,16},{4,20},{8,24},{12,28},{16,0},{20,4},{24,8},{28,12},{32,48},... | collective-permute-start | bytes 196616 | tf_op jit(solution)/shard_map/ppermute | solution.py:39
  203.9 9.0 %collective-permute-start.31 = (f32[128,128]{1,0:T(8,128)S(1)}, f32[128,128]{1,0:T(8,128)S(1)}, u32[]{:S(2)}, u32[]{:S(2)}) collective-permute-start(f32[128,128]{1,0:T(8,128)S(1)} %select_reduce_fusion.10), channel_id=1, source_target_pairs={{0,32},{4,36},{8,40},{12,44},{16,48},{20,52},{24,56},{28,60},{32,0... | collective-permute-start | bytes 196616 | tf_op jit(solution)/shard_map/ppermute | solution.py:28
  272.7 7.3 %collective-permute-start.35 = (bf16[128,3,256]{2,0,1:T(8,128)(2,1)S(1)}, bf16[128,3,256]{2,0,1:T(8,128)(2,1)S(1)}, u32[]{:S(2)}, u32[]{:S(2)}) collective-permute-start(bf16[128,3,256]{2,0,1:T(8,128)(2,1)S(1)} %get-tuple-element.25), channel_id=1, source_target_pairs={{0,4},{4,8},{8,12},{12,16},{16,20},{20,24},{24,28},{28,32},{32,36}... | collective-permute-start | bytes 589832 | tf_op jit(solution)/shard_map/ppermute | solution.py:17
  272.8 7.2 %collective-permute-start.36 = (bf16[128,3,256]{2,0,1:T(8,128)(2,1)S(1)}, bf16[128,3,256]{2,0,1:T(8,128)(2,1)S(1)}, u32[]{:S(2)}, u32[]{:S(2)}) collective-permute-start(bf16[128,3,256]{2,0,1:T(8,128)(2,1)S(1)} %get-tuple-element.26), channel_id=1, source_target_pairs={{4,0},{8,4},{12,8},{16,12},{20,16},{24,20},{28,24},{32,28},{36,32}... | collective-permute-start | bytes 589832 | tf_op jit(solution)/shard_map/ppermute | solution.py:19
  301.2 9.7 %collective-permute-start.37 = (f32[257,128]{1,0:T(8,128)S(1)}, f32[257,128]{1,0:T(8,128)S(1)}, u32[]{:S(2)}, u32[]{:S(2)}) collective-permute-start(f32[257,128]{1,0:T(8,128)S(1)} %get-tuple-element.32), channel_id=1, source_target_pairs={{0,1},{1,2},{2,3},{3,0},{4,5},{5,6},{6,7},{7,4},{8,9},{9,10},{10,1... | collective-permute-start | bytes 394760 | tf_op jit(solution)/shard_map/ppermute | solution.py:39
  301.6 9.3 %collective-permute-start.38 = (f32[257,128]{1,0:T(8,128)S(1)}, f32[257,128]{1,0:T(8,128)S(1)}, u32[]{:S(2)}, u32[]{:S(2)}) collective-permute-start(f32[257,128]{1,0:T(8,128)S(1)} %get-tuple-element.32), channel_id=1, source_target_pairs={{0,2},{1,3},{2,0},{3,1},{4,6},{5,7},{6,4},{7,5},{8,10},{9,11},{10,... | collective-permute-start | bytes 394760 | tf_op jit(solution)/shard_map/ppermute | solution.py:39
  304.3 7.2 %collective-permute-start.39 = (f32[257,128]{1,0:T(8,128)S(1)}, f32[257,128]{1,0:T(8,128)S(1)}, u32[]{:S(2)}, u32[]{:S(2)}) collective-permute-start(f32[257,128]{1,0:T(8,128)S(1)} %get-tuple-element.32), channel_id=1, source_target_pairs={{0,3},{1,0},{2,1},{3,2},{4,7},{5,4},{6,5},{7,6},{8,11},{9,8},{10,9... | collective-permute-start | bytes 394760 | tf_op jit(solution)/shard_map/ppermute | solution.py:39
  313.7 8.4 %collective-permute-start.41 = (f32[257,128]{1,0:T(8,128)S(1)}, f32[257,128]{1,0:T(8,128)S(1)}, u32[]{:S(2)}, u32[]{:S(2)}) collective-permute-start(f32[257,128]{1,0:T(8,128)S(1)} %add.229), channel_id=1, source_target_pairs={{0,8},{4,12},{8,16},{12,20},{16,24},{20,28},{24,0},{28,4},{32,40},... | collective-permute-start | bytes 394760 | tf_op jit(solution)/shard_map/ppermute | solution.py:39
  313.9 13.1 %collective-permute-start.42 = (f32[257,128]{1,0:T(8,128)S(1)}, f32[257,128]{1,0:T(8,128)S(1)}, u32[]{:S(2)}, u32[]{:S(2)}) collective-permute-start(f32[257,128]{1,0:T(8,128)S(1)} %add.229), channel_id=1, source_target_pairs={{0,16},{4,20},{8,24},{12,28},{16,0},{20,4},{24,8},{28,12},{32,48},... | collective-permute-start | bytes 394760 | tf_op jit(solution)/shard_map/ppermute | solution.py:39
  316.6 10.5 %collective-permute-start.43 = (f32[257,128]{1,0:T(8,128)S(1)}, f32[257,128]{1,0:T(8,128)S(1)}, u32[]{:S(2)}, u32[]{:S(2)}) collective-permute-start(f32[257,128]{1,0:T(8,128)S(1)} %add.229), channel_id=1, source_target_pairs={{0,24},{4,28},{8,0},{12,4},{16,8},{20,12},{24,16},{28,20},{32,56},... | collective-permute-start | bytes 394760 | tf_op jit(solution)/shard_map/ppermute | solution.py:39
  327.8 9.1 %collective-permute-start.44 = (f32[257,128]{1,0:T(8,128)S(1)}, f32[257,128]{1,0:T(8,128)S(1)}, u32[]{:S(2)}, u32[]{:S(2)}) collective-permute-start(f32[257,128]{1,0:T(8,128)S(1)} %select_reduce_fusion.1), channel_id=1, source_target_pairs={{0,32},{4,36},{8,40},{12,44},{16,48},{20,52},{24,56},{28,60},{32,0... | collective-permute-start | bytes 394760 | tf_op jit(solution)/shard_map/ppermute | solution.py:28
  339.6 6.8 %collective-permute-start.47 = (f32[257,128]{1,0:T(8,128)S(1)}, f32[257,128]{1,0:T(8,128)S(1)}, u32[]{:S(2)}, u32[]{:S(2)}) collective-permute-start(f32[257,128]{1,0:T(8,128)S(1)} %add.230), channel_id=1, source_target_pairs={{0,192},{4,196},{8,200},{12,204},{16,208},{20,212},{24,216},{28,22... | collective-permute-start | bytes 394760 | tf_op jit(solution)/shard_map/ppermute | solution.py:39
  358.6 9.0 %collective-permute-start.52 = (f32[128,128]{1,0:T(8,128)S(1)}, f32[128,128]{1,0:T(8,128)S(1)}, u32[]{:S(2)}, u32[]{:S(2)}) collective-permute-start(f32[128,128]{1,0:T(8,128)S(1)} %add.231), channel_id=1, source_target_pairs={{0,8},{4,12},{8,16},{12,20},{16,24},{20,28},{24,0},{28,4},{32,40},... | collective-permute-start | bytes 196616 | tf_op jit(solution)/shard_map/ppermute | solution.py:39
  371.9 8.3 %collective-permute-start.55 = (f32[128,128]{1,0:T(8,128)S(1)}, f32[128,128]{1,0:T(8,128)S(1)}, u32[]{:S(2)}, u32[]{:S(2)}) collective-permute-start(f32[128,128]{1,0:T(8,128)S(1)} %select_reduce_fusion.7), channel_id=1, source_target_pairs={{0,32},{4,36},{8,40},{12,44},{16,48},{20,52},{24,56},{28,60},{32,0... | collective-permute-start | bytes 196616 | tf_op jit(solution)/shard_map/ppermute | solution.py:28
  428.3 7.5 %collective-permute-start.66 = (f32[128]{0:T(128)S(1)}, f32[128]{0:T(128)S(1)}, u32[]{:S(2)}, u32[]{:S(2)}) collective-permute-start(f32[128]{0:T(128)S(1)} %select_reduce_fusion.17), channel_id=1, source_target_pairs={{0,32},{4,36},{8,40},{12,44},{16,48},{20,52},{24,56},{28,60},{32,0... | collective-permute-start | bytes 1544 | tf_op jit(solution)/shard_map/ppermute | solution.py:28
  435.8 11.1 %collective-permute-start.67 = (f32[128]{0:T(128)S(1)}, f32[128]{0:T(128)S(1)}, u32[]{:S(2)}, u32[]{:S(2)}) collective-permute-start(f32[128]{0:T(128)S(1)} %add.234), channel_id=1, source_target_pairs={{0,64},{4,68},{8,72},{12,76},{16,80},{20,84},{24,88},{28,92},{32,9... | collective-permute-start | bytes 1544 | tf_op jit(solution)/shard_map/ppermute | solution.py:39
  436.7 10.1 %collective-permute-start.68 = (f32[128]{0:T(128)S(1)}, f32[128]{0:T(128)S(1)}, u32[]{:S(2)}, u32[]{:S(2)}) collective-permute-start(f32[128]{0:T(128)S(1)} %add.234), channel_id=1, source_target_pairs={{0,128},{4,132},{8,136},{12,140},{16,144},{20,148},{24,152},{28,15... | collective-permute-start | bytes 1544 | tf_op jit(solution)/shard_map/ppermute | solution.py:39
  439.5 7.4 %collective-permute-start.69 = (f32[128]{0:T(128)S(1)}, f32[128]{0:T(128)S(1)}, u32[]{:S(2)}, u32[]{:S(2)}) collective-permute-start(f32[128]{0:T(128)S(1)} %add.234), channel_id=1, source_target_pairs={{0,192},{4,196},{8,200},{12,204},{16,208},{20,212},{24,216},{28,22... | collective-permute-start | bytes 1544 | tf_op jit(solution)/shard_map/ppermute | solution.py:39
  443.0 10.6 %all-to-all-start.1 = ((bf16[4,2,16384]{2,1,0:T(2,128)(2,1)}), bf16[4,2,16384]{2,1,0:T(2,128)(2,1)S(1)}, u32[]{:S(2)}, u32[]{:S(2)}) async-start(bf16[4,2,16384]{2,1,0:T(2,128)(2,1)} %reshape.450), calls=%async_computation.1 | async-start | bytes 524288 | tf_op jit(solution)/shard_map/all_to_all | solution.py:143
  (55 other events, 304.2 us)
Sparse Core Ops, SparseCore 0:
  85.9 29.1 all-gather.2
  246.9 24.1 all-gather.4
where the time goes:
time: 471 us; the launch traced here: 462 us
  waiting for transfers between devices  166 us (35%)
  starting transfers between devices  137 us (29%)
  other arithmetic  72.8 us (15%)
  local copies, waits for them, and re-layouts  50.1 us (11%)
  matrix products  21.2 us (5%)
  between operations  15.3 us (3%)
    ppermute x54, starting transfers between devices, group_step(): vals.append(lax.ppermute(x, axis, perm))  92.1 us
    ppermute x54, waiting for transfers between devices, group_step(): vals.append(lax.ppermute(x, axis, perm))  65.2 us
    all_gather x2, waiting for transfers between devices, local(): gathered = lax.all_gather(basis_cube, 'cols', axis=2, tiled=True)  53.5 us
    another operation x9, other arithmetic, orthonormal(): lower = jnp.linalg.cholesky(gram)  37.2 us
    another operation x6, other arithmetic, orthonormal(): jax.scipy.linalg.solve_triangular(lower, identity, lower=True)  31.4 us
    ppermute x12, waiting for transfers between devices, pair_step(): return x + lax.ppermute(x, axis, perm)  30.6 us
    ppermute x12, starting transfers between devices, pair_step(): return x + lax.ppermute(x, axis, perm)  28.4 us
    gather x16, local copies, waits for them, and re-layouts, fold_slots(): picked = jnp.take(piece, local_index[:, slot], axis=1)  23.6 us
  transfers between devices with their start and end apart: 74, of which 57 were waited for; matrix products, arithmetic and copies ran while one was open for 1% of the time, Pallas kernels for 0%

commit v1 on v0

--- a/solution.py
+++ b/solution.py
@@ -1,3 +1,4 @@
+import functools
 import math
 import jax
 import jax.numpy as jnp
@@ -5,6 +6,15 @@
 from jax.sharding import PartitionSpec as P
 
 REACH = 3
+
+
+def detail_joints_by_axis(payload, peer_axis):
+    return jnp.concatenate(
+        lax.all_to_all(jnp.stack(lax.axis_size(peer_axis) * [payload]), peer_axis, 0, 0), axis=2
+    )
+
+
+detail_numbers = functools.partial(detail_joints_by_axis, peer_axis="cols")
 
 
 def with_halo(cells, sides, width):
@@ -115,7 +125,7 @@
         image_count = basis_now.shape[0]
         basis_cube = basis_now.reshape(image_count, tiles_here, voxels_here)
         empty = jnp.zeros((image_count, tiles_here, voxels_here), jnp.float32)
-        gathered = lax.all_gather(basis_cube, "cols", axis=2, tiled=True)
+        gathered = detail_numbers(basis_cube)
         padded = with_halo(gathered, (("tiles", 1),), REACH)
         total = fold_slots(empty, padded, cov_blocks, local_index)
         image = (total * mask_values[None]).astype(jnp.bfloat16).reshape(image_count, -1)

time: 471 us -> 436 us (0.926)
  the two profiles are of different devices: /device:TPU:8 before, /device:TPU:32 now
where the time goes in v1:
time: 436 us; the launch traced here: 427 us
  waiting for transfers between devices  152 us (35%)
  starting transfers between devices  113 us (26%)
  other arithmetic  72.8 us (17%)
  local copies, waits for them, and re-layouts  49.8 us (11%)
  matrix products  21.2 us (5%)
  blocking collectives  16.3 us (4%)
    ppermute x54, waiting for transfers between devices, group_step(): vals.append(lax.ppermute(x, axis, perm))  82.2 us
    ppermute x54, starting transfers between devices, group_step(): vals.append(lax.ppermute(x, axis, perm))  74.9 us
    ppermute x12, waiting for transfers between devices, pair_step(): return x + lax.ppermute(x, axis, perm)  41.9 us
    another operation x9, other arithmetic, orthonormal(): lower = jnp.linalg.cholesky(gram)  37.2 us
    another operation x6, other arithmetic, orthonormal(): jax.scipy.linalg.solve_triangular(lower, identity, lower=True)  31.4 us
    gather x16, local copies, waits for them, and re-layouts, fold_slots(): picked = jnp.take(piece, local_index[:, slot], axis=1)  23.6 us
    ppermute x12, starting transfers between devices, pair_step(): return x + lax.ppermute(x, axis, perm)  22.5 us
    dot_general x16, matrix products, fold_slots(): jnp.einsum('iuv,biv->biu', blocks, picked, preferred_element_type=jnp.flo...  17.4 us
  transfers between devices with their start and end apart: 73, of which 61 were waited for; matrix products, arithmetic and copies ran while one was open for 1% of the time, Pallas kernels for 0%

profile of v1, /device:TPU:32, one launch (start us, length us, event | category | flops | bytes accessed | tf_op | source)
XLA Modules:
  0.0 427.3 jit_solution(5243140925792828616)
XLA Ops:
  4.7 4.3 %all-to-all-start = ((bf16[4,2,16384]{2,1,0:T(2,128)(2,1)}), bf16[4,2,16384]{2,1,0:T(2,128)(2,1)S(1)}, u32[]{:S(2)}, u32[]{:S(2)}) async-start(bf16[4,2,16384]{2,1,0:T(2,128)(2,1)} %reshape.460), calls=%async_computation | async-start | bytes 524288 | tf_op jit(solution)/shard_map/all_to_all | solution.py:114
  10.5 5.1 %all-to-all-done = bf16[4,2,16384]{2,1,0:T(2,128)(2,1)S(1)} async-done(((bf16[4,2,16384]{2,1,0:T(2,128)(2,1)}), bf16[4,2,16384]{2,1,0:T(2,128)(2,1)S(1)}, u32[]{:S(2)}, u32[]{:S(2)}) %all-to-all-start) | async-done | bytes 262176 | tf_op jit(solution)/shard_map/all_to_all | solution.py:114
  37.5 6.0 %collective-permute-start.7 = (f32[128,128]{1,0:T(8,128)S(1)}, f32[128,128]{1,0:T(8,128)S(1)}, u32[]{:S(2)}, u32[]{:S(2)}) collective-permute-start(f32[128,128]{1,0:T(8,128)S(1)} %select_reduce_fusion.13), channel_id=1, source_target_pairs={{0,32},{4,36},{8,40},{12,44},{16,48},{20,52},{24,56},{28,60},{32,0... | collective-permute-start | bytes 196616 | tf_op jit(solution)/shard_map/ppermute | solution.py:38
  43.5 3.6 collective-permute-done.7
  56.9 11.7 %cholesky.59 = f32[128,128]{1,0:T(8,128)S(1)} custom-call(f32[128,128]{1,0:T(8,128)S(1)} %fusion.122), custom_call_target="Cholesky" | custom-call | tf_op jit(solution)/shard_map/jit(cholesky)/cholesky | solution.py:85
  70.0 9.8 %custom-call.7 = f32[1,128,128]{1,2,0:T(8,128)S(1)} custom-call(f32[1,128,128]{2,1,0:T(8,128)S(1)} %fusion.114), custom_call_target="InvertDiagBlocksLowerTriangular" | custom-call | tf_op jit(solution)/shard_map/jit(_solve_triangular)/triangular_solve | solution.py:87
  81.8 3.7 all-to-all-start.1
  85.6 11.4 %all-to-all-done.1 = bf16[4,128,16,64]{1,3,2,0:T(8,128)(2,1)S(1)} async-done(((bf16[4,128,16,64]{1,3,2,0:T(8,128)(2,1)}), bf16[4,128,16,64]{1,3,2,0:T(8,128)(2,1)S(1)}, u32[]{:S(2)}, u32[]{:S(2)}) %all-to-all-start.1) | async-done | bytes 1048608 | tf_op jit(solution)/shard_map/all_to_all | solution.py:13
  129.4 3.5 collective-permute-done.13
  136.3 4.9 %collective-permute-start.18 = (f32[129,128]{1,0:T(8,128)S(1)}, f32[129,128]{1,0:T(8,128)S(1)}, u32[]{:S(2)}, u32[]{:S(2)}) collective-permute-start(f32[129,128]{1,0:T(8,128)S(1)} %add.217), channel_id=1, source_target_pairs={{0,16},{4,20},{8,24},{12,28},{16,0},{20,4},{24,8},{28,12},{32,48},... | collective-permute-start | bytes 198152 | tf_op jit(solution)/shard_map/ppermute | solution.py:49
  141.9 3.8 collective-permute-done.18
  148.1 4.6 %collective-permute-start.20 = (f32[129,128]{1,0:T(8,128)S(1)}, f32[129,128]{1,0:T(8,128)S(1)}, u32[]{:S(2)}, u32[]{:S(2)}) collective-permute-start(f32[129,128]{1,0:T(8,128)S(1)} %select_reduce_fusion.4), channel_id=1, source_target_pairs={{0,32},{4,36},{8,40},{12,44},{16,48},{20,52},{24,56},{28,60},{32,0... | collective-permute-start | bytes 198152 | tf_op jit(solution)/shard_map/ppermute | solution.py:38
  152.6 5.0 %collective-permute-done.20 = f32[129,128]{1,0:T(8,128)S(1)} collective-permute-done((f32[129,128]{1,0:T(8,128)S(1)}, f32[129,128]{1,0:T(8,128)S(1)}, u32[]{:S(2)}, u32[]{:S(2)}) %collective-permute-start.20) | collective-permute-done | bytes 66080 | tf_op jit(solution)/shard_map/ppermute | solution.py:38
  157.8 3.8 collective-permute-start.22
  167.5 3.8 collective-permute-start.25
  187.2 4.0 collective-permute-start.31
  191.3 5.4 %collective-permute-done.31 = f32[128,128]{1,0:T(8,128)S(1)} collective-permute-done((f32[128,128]{1,0:T(8,128)S(1)}, f32[128,128]{1,0:T(8,128)S(1)}, u32[]{:S(2)}, u32[]{:S(2)}) %collective-permute-start.31) | collective-permute-done | bytes 65568 | tf_op jit(solution)/shard_map/ppermute | solution.py:38
  205.2 11.7 %cholesky.70 = f32[128,128]{1,0:T(8,128)S(1)} custom-call(f32[128,128]{1,0:T(8,128)S(1)} %fusion.120), custom_call_target="Cholesky" | custom-call | tf_op jit(solution)/shard_map/jit(cholesky)/cholesky | solution.py:85
  218.2 9.8 %custom-call.8 = f32[1,128,128]{1,2,0:T(8,128)S(1)} custom-call(f32[1,128,128]{2,1,0:T(8,128)S(1)} %fusion.115), custom_call_target="InvertDiagBlocksLowerTriangular" | custom-call | tf_op jit(solution)/shard_map/jit(_solve_triangular)/triangular_solve | solution.py:87
  229.1 16.3 %all_to_all.37 = bf16[4,128,16,64]{1,3,2,0:T(8,128)(2,1)S(1)} all-to-all(bf16[4,128,16,64]{1,3,2,0:T(8,128)(2,1)S(1)} %stack.328), channel_id=1, replica_groups=mesh['tiles'=64,'cols'=4] {'cols'}, dimensions={0} | all-to-all | bytes 2097152 | tf_op jit(solution)/shard_map/all_to_all | solution.py:13
  278.2 3.2 collective-permute-done.37
  283.7 6.3 %collective-permute-start.42 = (f32[257,128]{1,0:T(8,128)S(1)}, f32[257,128]{1,0:T(8,128)S(1)}, u32[]{:S(2)}, u32[]{:S(2)}) collective-permute-start(f32[257,128]{1,0:T(8,128)S(1)} %add.229), channel_id=1, source_target_pairs={{0,16},{4,20},{8,24},{12,28},{16,0},{20,4},{24,8},{28,12},{32,48},... | collective-permute-start | bytes 394760 | tf_op jit(solution)/shard_map/ppermute | solution.py:49
  292.1 6.6 %collective-permute-done.42 = f32[257,128]{1,0:T(8,128)S(1)} collective-permute-done((f32[257,128]{1,0:T(8,128)S(1)}, f32[257,128]{1,0:T(8,128)S(1)}, u32[]{:S(2)}, u32[]{:S(2)}) %collective-permute-start.42) | collective-permute-done | bytes 131616 | tf_op jit(solution)/shard_map/ppermute | solution.py:49
  304.8 9.2 %collective-permute-done.44 = f32[257,128]{1,0:T(8,128)S(1)} collective-permute-done((f32[257,128]{1,0:T(8,128)S(1)}, f32[257,128]{1,0:T(8,128)S(1)}, u32[]{:S(2)}, u32[]{:S(2)}) %collective-permute-start.44) | collective-permute-done | bytes 131616 | tf_op jit(solution)/shard_map/ppermute | solution.py:38
  317.9 5.6 %collective-permute-done.45 = f32[257,128]{1,0:T(8,128)S(1)} collective-permute-done((f32[257,128]{1,0:T(8,128)S(1)}, f32[257,128]{1,0:T(8,128)S(1)}, u32[]{:S(2)}, u32[]{:S(2)}) %collective-permute-start.45) | collective-permute-done | bytes 131616 | tf_op jit(solution)/shard_map/ppermute | solution.py:49
  346.0 6.2 %collective-permute-done.55 = f32[128,128]{1,0:T(8,128)S(1)} collective-permute-done((f32[128,128]{1,0:T(8,128)S(1)}, f32[128,128]{1,0:T(8,128)S(1)}, u32[]{:S(2)}, u32[]{:S(2)}) %collective-permute-start.55) | collective-permute-done | bytes 65568 | tf_op jit(solution)/shard_map/ppermute | solution.py:38
  353.1 3.5 collective-permute-start.57
  361.8 11.7 %cholesky.81 = f32[128,128]{1,0:T(8,128)S(1)} custom-call(f32[128,128]{1,0:T(8,128)S(1)} %fusion.118), custom_call_target="Cholesky" | custom-call | tf_op jit(solution)/shard_map/jit(cholesky)/cholesky | solution.py:85
  374.9 9.8 %custom-call.9 = f32[1,128,128]{1,2,0:T(8,128)S(1)} custom-call(f32[1,128,128]{2,1,0:T(8,128)S(1)} %fusion.116), custom_call_target="InvertDiagBlocksLowerTriangular" | custom-call | tf_op jit(solution)/shard_map/jit(_solve_triangular)/triangular_solve | solution.py:87
  404.2 5.1 %collective-permute-done.66 = f32[128]{0:T(128)S(1)} collective-permute-done((f32[128]{0:T(128)S(1)}, f32[128]{0:T(128)S(1)}, u32[]{:S(2)}, u32[]{:S(2)}) %collective-permute-start.66) | collective-permute-done | bytes 544 | tf_op jit(solution)/shard_map/ppermute | solution.py:38
  415.2 3.4 all-to-all-start.3
  419.9 5.4 %all-to-all-done.3 = bf16[4,2,16384]{2,1,0:T(2,128)(2,1)S(1)} async-done(((bf16[4,2,16384]{2,1,0:T(2,128)(2,1)}), bf16[4,2,16384]{2,1,0:T(2,128)(2,1)S(1)}, u32[]{:S(2)}, u32[]{:S(2)}) %all-to-all-start.3) | async-done | bytes 262176 | tf_op jit(solution)/shard_map/all_to_all | solution.py:153
  (324 shorter events, 216.9 us)
Async XLA Ops:
  4.7 11.0 %all-to-all-start = ((bf16[4,2,16384]{2,1,0:T(2,128)(2,1)}), bf16[4,2,16384]{2,1,0:T(2,128)(2,1)S(1)}, u32[]{:S(2)}, u32[]{:S(2)}) async-start(bf16[4,2,16384]{2,1,0:T(2,128)(2,1)} %reshape.460), calls=%async_computation | async-start | bytes 524288 | tf_op jit(solution)/shard_map/all_to_all | solution.py:114
  30.2 6.5 %collective-permute-start.6 = (f32[128,128]{1,0:T(8,128)S(1)}, f32[128,128]{1,0:T(8,128)S(1)}, u32[]{:S(2)}, u32[]{:S(2)}) collective-permute-start(f32[128,128]{1,0:T(8,128)S(1)} %add.200), channel_id=1, source_target_pairs={{0,24},{4,28},{8,0},{12,4},{16,8},{20,12},{24,16},{28,20},{32,56},... | collective-permute-start | bytes 196616 | tf_op jit(solution)/shard_map/ppermute | solution.py:49
  37.5 9.6 %collective-permute-start.7 = (f32[128,128]{1,0:T(8,128)S(1)}, f32[128,128]{1,0:T(8,128)S(1)}, u32[]{:S(2)}, u32[]{:S(2)}) collective-permute-start(f32[128,128]{1,0:T(8,128)S(1)} %select_reduce_fusion.13), channel_id=1, source_target_pairs={{0,32},{4,36},{8,40},{12,44},{16,48},{20,52},{24,56},{28,60},{32,0... | collective-permute-start | bytes 196616 | tf_op jit(solution)/shard_map/ppermute | solution.py:38
  47.1 6.4 %collective-permute-start.8 = (f32[128,128]{1,0:T(8,128)S(1)}, f32[128,128]{1,0:T(8,128)S(1)}, u32[]{:S(2)}, u32[]{:S(2)}) collective-permute-start(f32[128,128]{1,0:T(8,128)S(1)} %add.203), channel_id=1, source_target_pairs={{0,64},{4,68},{8,72},{12,76},{16,80},{20,84},{24,88},{28,92},{32,9... | collective-permute-start | bytes 196616 | tf_op jit(solution)/shard_map/ppermute | solution.py:49
  81.8 15.2 %all-to-all-start.1 = ((bf16[4,128,16,64]{1,3,2,0:T(8,128)(2,1)}), bf16[4,128,16,64]{1,3,2,0:T(8,128)(2,1)S(1)}, u32[]{:S(2)}, u32[]{:S(2)}) async-start(bf16[4,128,16,64]{1,3,2,0:T(8,128)(2,1)} %stack.297), calls=%async_computation.1 | async-start | bytes 2097152 | tf_op jit(solution)/shard_map/all_to_all | solution.py:13
  126.0 6.9 %collective-permute-start.13 = (f32[129,128]{1,0:T(8,128)S(1)}, f32[129,128]{1,0:T(8,128)S(1)}, u32[]{:S(2)}, u32[]{:S(2)}) collective-permute-start(f32[129,128]{1,0:T(8,128)S(1)} %get-tuple-element.34), channel_id=1, source_target_pairs={{0,1},{1,2},{2,3},{3,0},{4,5},{5,6},{6,7},{7,4},{8,9},{9,10},{10,1... | collective-permute-start | bytes 198152 | tf_op jit(solution)/shard_map/ppermute | solution.py:49
  126.6 6.3 %collective-permute-start.14 = (f32[129,128]{1,0:T(8,128)S(1)}, f32[129,128]{1,0:T(8,128)S(1)}, u32[]{:S(2)}, u32[]{:S(2)}) collective-permute-start(f32[129,128]{1,0:T(8,128)S(1)} %get-tuple-element.34), channel_id=1, source_target_pairs={{0,2},{1,3},{2,0},{3,1},{4,6},{5,7},{6,4},{7,5},{8,10},{9,11},{10,... | collective-permute-start | bytes 198152 | tf_op jit(solution)/shard_map/ppermute | solution.py:49
  135.5 6.4 %collective-permute-start.17 = (f32[129,128]{1,0:T(8,128)S(1)}, f32[129,128]{1,0:T(8,128)S(1)}, u32[]{:S(2)}, u32[]{:S(2)}) collective-permute-start(f32[129,128]{1,0:T(8,128)S(1)} %add.217), channel_id=1, source_target_pairs={{0,8},{4,12},{8,16},{12,20},{16,24},{20,28},{24,0},{28,4},{32,40},... | collective-permute-start | bytes 198152 | tf_op jit(solution)/shard_map/ppermute | solution.py:49
  136.3 9.4 %collective-permute-start.18 = (f32[129,128]{1,0:T(8,128)S(1)}, f32[129,128]{1,0:T(8,128)S(1)}, u32[]{:S(2)}, u32[]{:S(2)}) collective-permute-start(f32[129,128]{1,0:T(8,128)S(1)} %add.217), channel_id=1, source_target_pairs={{0,16},{4,20},{8,24},{12,28},{16,0},{20,4},{24,8},{28,12},{32,48},... | collective-permute-start | bytes 198152 | tf_op jit(solution)/shard_map/ppermute | solution.py:49
  148.1 9.6 %collective-permute-start.20 = (f32[129,128]{1,0:T(8,128)S(1)}, f32[129,128]{1,0:T(8,128)S(1)}, u32[]{:S(2)}, u32[]{:S(2)}) collective-permute-start(f32[129,128]{1,0:T(8,128)S(1)} %select_reduce_fusion.4), channel_id=1, source_target_pairs={{0,32},{4,36},{8,40},{12,44},{16,48},{20,52},{24,56},{28,60},{32,0... | collective-permute-start | bytes 198152 | tf_op jit(solution)/shard_map/ppermute | solution.py:38
  157.8 6.8 %collective-permute-start.22 = (f32[129,128]{1,0:T(8,128)S(1)}, f32[129,128]{1,0:T(8,128)S(1)}, u32[]{:S(2)}, u32[]{:S(2)}) collective-permute-start(f32[129,128]{1,0:T(8,128)S(1)} %add.218), channel_id=1, source_target_pairs={{0,128},{4,132},{8,136},{12,140},{16,144},{20,148},{24,152},{28,15... | collective-permute-start | bytes 198152 | tf_op jit(solution)/shard_map/ppermute | solution.py:49
  167.5 6.8 %collective-permute-start.25 = (f32[128,128]{1,0:T(8,128)S(1)}, f32[128,128]{1,0:T(8,128)S(1)}, u32[]{:S(2)}, u32[]{:S(2)}) collective-permute-start(f32[128,128]{1,0:T(8,128)S(1)} %fusion.155), channel_id=1, source_target_pairs={{0,2},{1,3},{2,0},{3,1},{4,6},{5,7},{6,4},{7,5},{8,10},{9,11},{10,... | collective-permute-start | bytes 196616 | tf_op jit(solution)/shard_map/ppermute | solution.py:49
  177.8 6.7 %collective-permute-start.29 = (f32[128,128]{1,0:T(8,128)S(1)}, f32[128,128]{1,0:T(8,128)S(1)}, u32[]{:S(2)}, u32[]{:S(2)}) collective-permute-start(f32[128,128]{1,0:T(8,128)S(1)} %add.219), channel_id=1, source_target_pairs={{0,16},{4,20},{8,24},{12,28},{16,0},{20,4},{24,8},{28,12},{32,48},... | collective-permute-start | bytes 196616 | tf_op jit(solution)/shard_map/ppermute | solution.py:49
  180.2 6.3 %collective-permute-start.30 = (f32[128,128]{1,0:T(8,128)S(1)}, f32[128,128]{1,0:T(8,128)S(1)}, u32[]{:S(2)}, u32[]{:S(2)}) collective-permute-start(f32[128,128]{1,0:T(8,128)S(1)} %add.219), channel_id=1, source_target_pairs={{0,24},{4,28},{8,0},{12,4},{16,8},{20,12},{24,16},{28,20},{32,56},... | collective-permute-start | bytes 196616 | tf_op jit(solution)/shard_map/ppermute | solution.py:49
  187.2 9.4 %collective-permute-start.31 = (f32[128,128]{1,0:T(8,128)S(1)}, f32[128,128]{1,0:T(8,128)S(1)}, u32[]{:S(2)}, u32[]{:S(2)}) collective-permute-start(f32[128,128]{1,0:T(8,128)S(1)} %select_reduce_fusion.10), channel_id=1, source_target_pairs={{0,32},{4,36},{8,40},{12,44},{16,48},{20,52},{24,56},{28,60},{32,0... | collective-permute-start | bytes 196616 | tf_op jit(solution)/shard_map/ppermute | solution.py:38
  273.7 7.7 %collective-permute-start.37 = (f32[257,128]{1,0:T(8,128)S(1)}, f32[257,128]{1,0:T(8,128)S(1)}, u32[]{:S(2)}, u32[]{:S(2)}) collective-permute-start(f32[257,128]{1,0:T(8,128)S(1)} %get-tuple-element.32), channel_id=1, source_target_pairs={{0,1},{1,2},{2,3},{3,0},{4,5},{5,6},{6,7},{7,4},{8,9},{9,10},{10,1... | collective-permute-start | bytes 394760 | tf_op jit(solution)/shard_map/ppermute | solution.py:49
  274.6 6.8 %collective-permute-start.38 = (f32[257,128]{1,0:T(8,128)S(1)}, f32[257,128]{1,0:T(8,128)S(1)}, u32[]{:S(2)}, u32[]{:S(2)}) collective-permute-start(f32[257,128]{1,0:T(8,128)S(1)} %get-tuple-element.32), channel_id=1, source_target_pairs={{0,2},{1,3},{2,0},{3,1},{4,6},{5,7},{6,4},{7,5},{8,10},{9,11},{10,... | collective-permute-start | bytes 394760 | tf_op jit(solution)/shard_map/ppermute | solution.py:49
  283.6 8.5 %collective-permute-start.41 = (f32[257,128]{1,0:T(8,128)S(1)}, f32[257,128]{1,0:T(8,128)S(1)}, u32[]{:S(2)}, u32[]{:S(2)}) collective-permute-start(f32[257,128]{1,0:T(8,128)S(1)} %add.229), channel_id=1, source_target_pairs={{0,8},{4,12},{8,16},{12,20},{16,24},{20,28},{24,0},{28,4},{32,40},... | collective-permute-start | bytes 394760 | tf_op jit(solution)/shard_map/ppermute | solution.py:49
  283.7 15.0 %collective-permute-start.42 = (f32[257,128]{1,0:T(8,128)S(1)}, f32[257,128]{1,0:T(8,128)S(1)}, u32[]{:S(2)}, u32[]{:S(2)}) collective-permute-start(f32[257,128]{1,0:T(8,128)S(1)} %add.229), channel_id=1, source_target_pairs={{0,16},{4,20},{8,24},{12,28},{16,0},{20,4},{24,8},{28,12},{32,48},... | collective-permute-start | bytes 394760 | tf_op jit(solution)/shard_map/ppermute | solution.py:49
  290.0 11.5 %collective-permute-start.43 = (f32[257,128]{1,0:T(8,128)S(1)}, f32[257,128]{1,0:T(8,128)S(1)}, u32[]{:S(2)}, u32[]{:S(2)}) collective-permute-start(f32[257,128]{1,0:T(8,128)S(1)} %add.229), channel_id=1, source_target_pairs={{0,24},{4,28},{8,0},{12,4},{16,8},{20,12},{24,16},{28,20},{32,56},... | collective-permute-start | bytes 394760 | tf_op jit(solution)/shard_map/ppermute | solution.py:49
  302.3 11.7 %collective-permute-start.44 = (f32[257,128]{1,0:T(8,128)S(1)}, f32[257,128]{1,0:T(8,128)S(1)}, u32[]{:S(2)}, u32[]{:S(2)}) collective-permute-start(f32[257,128]{1,0:T(8,128)S(1)} %select_reduce_fusion.1), channel_id=1, source_target_pairs={{0,32},{4,36},{8,40},{12,44},{16,48},{20,52},{24,56},{28,60},{32,0... | collective-permute-start | bytes 394760 | tf_op jit(solution)/shard_map/ppermute | solution.py:38
  314.0 9.5 %collective-permute-start.45 = (f32[257,128]{1,0:T(8,128)S(1)}, f32[257,128]{1,0:T(8,128)S(1)}, u32[]{:S(2)}, u32[]{:S(2)}) collective-permute-start(f32[257,128]{1,0:T(8,128)S(1)} %add.230), channel_id=1, source_target_pairs={{0,64},{4,68},{8,72},{12,76},{16,80},{20,84},{24,88},{28,92},{32,9... | collective-permute-start | bytes 394760 | tf_op jit(solution)/shard_map/ppermute | solution.py:49
  314.1 9.4 %collective-permute-start.46 = (f32[257,128]{1,0:T(8,128)S(1)}, f32[257,128]{1,0:T(8,128)S(1)}, u32[]{:S(2)}, u32[]{:S(2)}) collective-permute-start(f32[257,128]{1,0:T(8,128)S(1)} %add.230), channel_id=1, source_target_pairs={{0,128},{4,132},{8,136},{12,140},{16,144},{20,148},{24,152},{28,15... | collective-permute-start | bytes 394760 | tf_op jit(solution)/shard_map/ppermute | solution.py:49
  316.6 7.4 %collective-permute-start.47 = (f32[257,128]{1,0:T(8,128)S(1)}, f32[257,128]{1,0:T(8,128)S(1)}, u32[]{:S(2)}, u32[]{:S(2)}) collective-permute-start(f32[257,128]{1,0:T(8,128)S(1)} %add.230), channel_id=1, source_target_pairs={{0,192},{4,196},{8,200},{12,204},{16,208},{20,212},{24,216},{28,22... | collective-permute-start | bytes 394760 | tf_op jit(solution)/shard_map/ppermute | solution.py:49
  334.9 7.8 %collective-permute-start.54 = (f32[128,128]{1,0:T(8,128)S(1)}, f32[128,128]{1,0:T(8,128)S(1)}, u32[]{:S(2)}, u32[]{:S(2)}) collective-permute-start(f32[128,128]{1,0:T(8,128)S(1)} %add.231), channel_id=1, source_target_pairs={{0,24},{4,28},{8,0},{12,4},{16,8},{20,12},{24,16},{28,20},{32,56},... | collective-permute-start | bytes 196616 | tf_op jit(solution)/shard_map/ppermute | solution.py:49
  343.5 8.7 %collective-permute-start.55 = (f32[128,128]{1,0:T(8,128)S(1)}, f32[128,128]{1,0:T(8,128)S(1)}, u32[]{:S(2)}, u32[]{:S(2)}) collective-permute-start(f32[128,128]{1,0:T(8,128)S(1)} %select_reduce_fusion.7), channel_id=1, source_target_pairs={{0,32},{4,36},{8,40},{12,44},{16,48},{20,52},{24,56},{28,60},{32,0... | collective-permute-start | bytes 196616 | tf_op jit(solution)/shard_map/ppermute | solution.py:38
  353.1 6.6 %collective-permute-start.57 = (f32[128,128]{1,0:T(8,128)S(1)}, f32[128,128]{1,0:T(8,128)S(1)}, u32[]{:S(2)}, u32[]{:S(2)}) collective-permute-start(f32[128,128]{1,0:T(8,128)S(1)} %add.232), channel_id=1, source_target_pairs={{0,128},{4,132},{8,136},{12,140},{16,144},{20,148},{24,152},{28,15... | collective-permute-start | bytes 196616 | tf_op jit(solution)/shard_map/ppermute | solution.py:49
  401.8 7.5 %collective-permute-start.66 = (f32[128]{0:T(128)S(1)}, f32[128]{0:T(128)S(1)}, u32[]{:S(2)}, u32[]{:S(2)}) collective-permute-start(f32[128]{0:T(128)S(1)} %select_reduce_fusion.17), channel_id=1, source_target_pairs={{0,32},{4,36},{8,40},{12,44},{16,48},{20,52},{24,56},{28,60},{32,0... | collective-permute-start | bytes 1544 | tf_op jit(solution)/shard_map/ppermute | solution.py:38
  409.3 9.3 %collective-permute-start.67 = (f32[128]{0:T(128)S(1)}, f32[128]{0:T(128)S(1)}, u32[]{:S(2)}, u32[]{:S(2)}) collective-permute-start(f32[128]{0:T(128)S(1)} %add.234), channel_id=1, source_target_pairs={{0,64},{4,68},{8,72},{12,76},{16,80},{20,84},{24,88},{28,92},{32,9... | collective-permute-start | bytes 1544 | tf_op jit(solution)/shard_map/ppermute | solution.py:49
  409.5 9.1 %collective-permute-start.68 = (f32[128]{0:T(128)S(1)}, f32[128]{0:T(128)S(1)}, u32[]{:S(2)}, u32[]{:S(2)}) collective-permute-start(f32[128]{0:T(128)S(1)} %add.234), channel_id=1, source_target_pairs={{0,128},{4,132},{8,136},{12,140},{16,144},{20,148},{24,152},{28,15... | collective-permute-start | bytes 1544 | tf_op jit(solution)/shard_map/ppermute | solution.py:49
  412.2 6.5 %collective-permute-start.69 = (f32[128]{0:T(128)S(1)}, f32[128]{0:T(128)S(1)}, u32[]{:S(2)}, u32[]{:S(2)}) collective-permute-start(f32[128]{0:T(128)S(1)} %add.234), channel_id=1, source_target_pairs={{0,192},{4,196},{8,200},{12,204},{16,208},{20,212},{24,216},{28,22... | collective-permute-start | bytes 1544 | tf_op jit(solution)/shard_map/ppermute | solution.py:49
  415.2 10.1 %all-to-all-start.3 = ((bf16[4,2,16384]{2,1,0:T(2,128)(2,1)}), bf16[4,2,16384]{2,1,0:T(2,128)(2,1)S(1)}, u32[]{:S(2)}, u32[]{:S(2)}) async-start(bf16[4,2,16384]{2,1,0:T(2,128)(2,1)} %reshape.462), calls=%async_computation.3 | async-start | bytes 524288 | tf_op jit(solution)/shard_map/all_to_all | solution.py:153
  (54 other events, 276.9 us)
